TPU v7x, 32 devices: a whole 2x2x4 slice. The times are simulated.
32 devices in a mesh: group: 2 (over core), gx: 4 (over y, x), gy: 4 (over z).
Axes of the slice: x: 2, y: 2, z: 4, core: 2. Of those that a mesh axis runs over, the one named last changes fastest.
Arguments:
- gradient_windows: bfloat16 [2, 4, 4, 256, 4, 2, 128], P('group', 'gx', 'gy'), may hold values from -6 to 6
- illumination_windows: bfloat16 [2, 4, 4, 256, 4, 2, 128], P('group', 'gx', 'gy'), may hold values from 0.25 to 8
- window_owners: int32 [2, 4, 4, 256], P('group', 'gx', 'gy'), may hold values from 0 to 15, as said below
- window_patches: int32 [2, 4, 4, 256], P('group', 'gx', 'gy'), may hold values from 0 to 7
- velocity: float32 [4, 64, 512], P(None, 'gx', 'gy'), may hold values from 1.5 to 4.5
Outputs:
- updated_model: float32 [4, 64, 512], P(None, 'gx', 'gy')
- returned_windows: bfloat16 [2, 4, 4, 256, 4, 2, 128], P('group', 'gx', 'gy')
Inputs may be any that keep to these rules, and one draw needn't show every extreme that they name: `window_owners`: the window patches of one device name any tile at most 20 times; one tile is named exactly 20 times by the window patches of every device.
All inputs are finite; a program needn't handle non-finite values.
Results may differ from a plain program's by a relative error of at most 0.001.
Values may be sent and summed in bfloat16 or wider, within the bound.
No kernel may reach another device: no remote copies, remote signals or barrier semaphores. Data moves between devices by JAX's collectives and lax.ppermute only.
A program may use at most 64 MiB of HBM per device.

v0:
```python
import jax
import jax.numpy as jnp
from jax import lax
from jax.sharding import PartitionSpec as P

SWEEPS = 4
damping = 10.0
smooth_rate = 0.12
step_length = 24.0


def with_halo(cells, sides, width):
    for axis, dim in sides:
        count = lax.axis_size(axis)
        ends = count - 1
        head = lax.slice_in_dim(cells, 0, width, axis=dim)
        tail = lax.slice_in_dim(cells, cells.shape[dim] - width, cells.shape[dim], axis=dim)
        cells = jnp.concatenate(
            [
                lax.ppermute(tail, axis, [(i, (i + 1) % count) for i in range(ends)]),
                cells,
                lax.ppermute(head, axis, [((i + 1) % count, i) for i in range(ends)]),
            ],
            axis=dim,
        )
    return cells


def deliver(send_grad, send_illum, send_patch, size_x, size_y, capacity):
    sectioned_grad = send_grad.reshape((size_x, size_y, capacity) + send_grad.shape[1:])
    sectioned_illum = send_illum.reshape((size_x, size_y, capacity) + send_illum.shape[1:])
    sectioned_patch = send_patch.reshape(size_x, size_y, capacity)
    got_grad, got_illum, got_patch = (
        lax.all_to_all(
            lax.all_to_all(sectioned_grad, "gx", split_axis=0, concat_axis=0, tiled=True),
            "gy",
            split_axis=1,
            concat_axis=1,
            tiled=True,
        ),
        lax.all_to_all(
            lax.all_to_all(sectioned_illum, "gx", split_axis=0, concat_axis=0, tiled=True),
            "gy",
            split_axis=1,
            concat_axis=1,
            tiled=True,
        ),
        lax.all_to_all(
            lax.all_to_all(sectioned_patch, "gx", split_axis=0, concat_axis=0, tiled=True),
            "gy",
            split_axis=1,
            concat_axis=1,
            tiled=True,
        ),
    )
    return (
        got_grad.reshape(send_grad.shape),
        got_illum.reshape(send_illum.shape),
        got_patch.reshape(send_patch.shape),
    )


def send_back(back_rows, size_x, size_y, capacity):
    sectioned_back = back_rows.reshape((size_x, size_y, capacity) + back_rows.shape[1:])
    arrived = lax.all_to_all(
        lax.all_to_all(sectioned_back, "gx", split_axis=0, concat_axis=0, tiled=True),
        "gy",
        split_axis=1,
        concat_axis=1,
        tiled=True,
    )
    return arrived.reshape(back_rows.shape)


def smooth_whole(field_now):
    for sweep_index in range(SWEEPS):
        padded = with_halo(field_now, (("gx", 1), ("gy", 2)), 1)
        depth_pad = jnp.pad(field_now, ((1, 1), (0, 0), (0, 0)))
        beside = (
            padded[:, 2:, 1:-1]
            + padded[:, :-2, 1:-1]
            + (padded[:, 1:-1, 2:] + padded[:, 1:-1, :-2])
            + (depth_pad[2:] + depth_pad[:-2])
        )
        field_now = field_now + smooth_rate * (beside - 6.0 * field_now)
    return field_now


def local(gradient_windows, illumination_windows, window_owners, window_patches, velocity):
    size_x = lax.axis_size("gx")
    size_y = lax.axis_size("gy")
    holder_count = size_x * size_y
    slot_grad = gradient_windows[0, 0, 0]
    slot_illum = illumination_windows[0, 0, 0]
    owners = window_owners[0, 0, 0]
    patches = window_patches[0, 0, 0]
    slot_count, levels, patch_rows, patch_cols = slot_grad.shape
    patch_count = velocity.shape[1] // patch_rows
    mean_load = slot_count // holder_count
    capacity = mean_load + max(1, slot_count // (4 * holder_count))
    rows_total = holder_count * capacity
    cell_count = levels * patch_rows * patch_cols
    member = (owners[:, None] == jnp.arange(holder_count, dtype=jnp.int32)[None, :]).astype(
        jnp.int32
    )
    slot_rank = jnp.sum(jnp.cumsum(member, axis=0) * member, axis=1) - 1
    position = owners * capacity + slot_rank
    send_grad = (
        jnp.zeros((rows_total, levels, patch_rows, patch_cols), jnp.bfloat16)
        .at[position]
        .set(slot_grad)
    )
    send_illum = (
        jnp.zeros((rows_total, levels, patch_rows, patch_cols), jnp.bfloat16)
        .at[position]
        .set(slot_illum)
    )
    send_patch = jnp.full((rows_total,), -1, jnp.int32).at[position].set(patches)
    got_grad, got_illum, got_patch = deliver(
        send_grad, send_illum, send_patch, size_x, size_y, capacity
    )
    onehot = (got_patch[None, :] == jnp.arange(patch_count, dtype=jnp.int32)[:, None]).astype(
        jnp.bfloat16
    )
    grad_sum = jnp.dot(
        onehot, got_grad.reshape(rows_total, cell_count), preferred_element_type=jnp.float32
    )
    illum_sum = jnp.dot(
        onehot, got_illum.reshape(rows_total, cell_count), preferred_element_type=jnp.float32
    )

    def to_tile(patch_sums):
        return (
            patch_sums.reshape(patch_count, levels, patch_rows, patch_cols)
            .transpose(1, 0, 2, 3)
            .reshape(levels, patch_count * patch_rows, patch_cols)
        )

    grad_total, illum_total = lax.psum((to_tile(grad_sum), to_tile(illum_sum)), "group")
    smoothed = smooth_whole(grad_total / (illum_total + damping))
    updated_model = velocity - step_length * smoothed
    patch_table = (
        updated_model.reshape(levels, patch_count, patch_rows, patch_cols)
        .transpose(1, 0, 2, 3)
        .reshape(patch_count, cell_count)
        .astype(jnp.bfloat16)
    )
    back_rows = jnp.dot(onehot.T, patch_table, preferred_element_type=jnp.float32).astype(
        jnp.bfloat16
    )
    back_rows = back_rows.reshape(rows_total, levels, patch_rows, patch_cols)
    arrived = send_back(back_rows, size_x, size_y, capacity)
    returned = jnp.take(arrived, position, axis=0)
    returned_windows = returned.reshape((1, 1, 1) + returned.shape)
    return (updated_model, returned_windows)


def solution(mesh):
    return jax.shard_map(
        local,
        mesh=mesh,
        in_specs=(
            P("group", "gx", "gy", None, None, None, None),
            P("group", "gx", "gy", None, None, None, None),
            P("group", "gx", "gy", None),
            P("group", "gx", "gy", None),
            P(None, "gx", "gy"),
        ),
        out_specs=(P(None, "gx", "gy"), P("group", "gx", "gy", None, None, None, None)),
        check_vma=False,
    )
```

profile of v0, /device:TPU:0, one launch (start us, length us, event | category | flops | bytes accessed | tf_op | source)
XLA Modules:
  0.0 227.5 jit_solution(14534622303721739606)
XLA Ops:
  10.1 1.6 scatter_custom_fusion
  11.8 9.7 %all_to_all.40 = s32[4,4,20]{2,1,0:T(4,128)S(1)} all-to-all(s32[4,4,20]{2,1,0:T(4,128)S(1)} %reshape.97), channel_id=1, replica_groups=mesh['group'=2,'gx'=4,'gy'=4] {'gx'}, dimensions={0} | all-to-all | bytes 2560 | tf_op jit(solution)/shard_map/all_to_all | solution.py:49
  22.0 4.9 %all-to-all-start.1 = ((s32[4,4,20]{2,0,1:T(4,128)}), s32[4,4,20]{2,0,1:T(4,128)S(1)}, u32[]{:S(2)}, u32[]{:S(2)}) async-start(s32[4,4,20]{2,0,1:T(4,128)} %copy.49), calls=%async_computation.1 | async-start | bytes 16384 | tf_op jit(solution)/shard_map/all_to_all | solution.py:48
  26.9 1.2 copy.57
  28.3 7.1 %scatter_fusion.1 = bf16[320,4,2,128]{3,1,2,0:T(4,128)(2,1)S(1)} fusion(bf16[320,4,2,128]{3,1,2,0:T(4,128)(2,1)S(1)} %broadcast.109.clone.1, s32[256]{0:T(256)S(1)} %bitcast.69, bf16[256,4,2,128]{3,1,2,0:T(4,128)(2,1)S(1)} %copy.57), kind=kCustom, calls=%fused_computation.3 | custom fusion | bytes 1573888 | tf_op jit(solution)/shard_map/scatter | solution.py:116
  35.4 1.5 copy.58
  36.9 3.6 %all-to-all-start.4 = ((bf16[4,4,20,4,2,128]{5,4,3,2,1,0:T(2,128)(2,1)}), bf16[4,4,20,4,2,128]{5,4,3,2,1,0:T(2,128)(2,1)S(1)}, u32[]{:S(2)}, u32[]{:S(2)}) async-start(bf16[4,4,20,4,2,128]{5,4,3,2,1,0:T(2,128)(2,1)} %copy.58), calls=%async_computation.4 | async-start | bytes 1310720 | tf_op jit(solution)/shard_map/all_to_all | solution.py:42
  40.9 7.1 %scatter_fusion = bf16[320,4,2,128]{3,1,2,0:T(4,128)(2,1)S(1)} fusion(bf16[320,4,2,128]{3,1,2,0:T(4,128)(2,1)S(1)} %broadcast.109.clone, s32[256]{0:T(256)S(1)} %bitcast.70, bf16[256,4,2,128]{3,1,2,0:T(4,128)(2,1)S(1)} %copy.51), kind=kCustom, calls=%fused_computation.2 | custom fusion | bytes 1573888 | tf_op jit(solution)/shard_map/scatter | solution.py:111
  48.0 1.5 copy.52
  49.5 4.1 %all-to-all-start.2 = ((bf16[4,4,20,4,2,128]{5,4,3,2,1,0:T(2,128)(2,1)}), bf16[4,4,20,4,2,128]{5,4,3,2,1,0:T(2,128)(2,1)S(1)}, u32[]{:S(2)}, u32[]{:S(2)}) async-start(bf16[4,4,20,4,2,128]{5,4,3,2,1,0:T(2,128)(2,1)} %copy.52), calls=%async_computation.2 | async-start | bytes 1310720 | tf_op jit(solution)/shard_map/all_to_all | solution.py:35
  53.7 1.3 copy.59
  55.0 6.1 %all-to-all-done.2 = bf16[4,4,20,4,2,128]{5,4,3,2,1,0:T(2,128)(2,1)S(1)} async-done(((bf16[4,4,20,4,2,128]{5,4,3,2,1,0:T(2,128)(2,1)}), bf16[4,4,20,4,2,128]{5,4,3,2,1,0:T(2,128)(2,1)S(1)}, u32[]{:S(2)}, u32[]{:S(2)}) %all-to-all-start.2) | async-done | bytes 655392 | tf_op jit(solution)/shard_map/all_to_all | solution.py:35
  61.1 4.9 %all-to-all-start.5 = ((bf16[4,4,20,4,2,128]{5,4,3,2,0,1:T(2,128)(2,1)}), bf16[4,4,20,4,2,128]{5,4,3,2,0,1:T(2,128)(2,1)S(1)}, u32[]{:S(2)}, u32[]{:S(2)}) async-start(bf16[4,4,20,4,2,128]{5,4,3,2,0,1:T(2,128)(2,1)} %copy.59), calls=%async_computation.5 | async-start | bytes 1310720 | tf_op jit(solution)/shard_map/all_to_all | solution.py:41
  66.1 1.3 copy.53
  67.4 12.3 %all-to-all-done.5 = bf16[4,4,20,4,2,128]{5,4,3,2,0,1:T(2,128)(2,1)S(1)} async-done(((bf16[4,4,20,4,2,128]{5,4,3,2,0,1:T(2,128)(2,1)}), bf16[4,4,20,4,2,128]{5,4,3,2,0,1:T(2,128)(2,1)S(1)}, u32[]{:S(2)}, u32[]{:S(2)}) %all-to-all-start.5) | async-done | bytes 655392 | tf_op jit(solution)/shard_map/all_to_all | solution.py:41
  79.7 3.5 %all-to-all-start.3 = ((bf16[4,4,20,4,2,128]{5,4,3,2,0,1:T(2,128)(2,1)}), bf16[4,4,20,4,2,128]{5,4,3,2,0,1:T(2,128)(2,1)S(1)}, u32[]{:S(2)}, u32[]{:S(2)}) async-start(bf16[4,4,20,4,2,128]{5,4,3,2,0,1:T(2,128)(2,1)} %copy.53), calls=%async_computation.3 | async-start | bytes 1310720 | tf_op jit(solution)/shard_map/all_to_all | solution.py:34
  85.6 12.3 %all-to-all-done.3 = bf16[4,4,20,4,2,128]{5,4,3,2,0,1:T(2,128)(2,1)S(1)} async-done(((bf16[4,4,20,4,2,128]{5,4,3,2,0,1:T(2,128)(2,1)}), bf16[4,4,20,4,2,128]{5,4,3,2,0,1:T(2,128)(2,1)S(1)}, u32[]{:S(2)}, u32[]{:S(2)}) %all-to-all-start.3) | async-done | bytes 655392 | tf_op jit(solution)/shard_map/all_to_all | solution.py:34
  100.1 16.3 %all-reduce.7.cloned.1.call-done = (f32[4,16,128]{2,1,0:T(8,128)}, f32[4,16,128]{2,1,0:T(8,128)}) async-done(((f32[4,16,128]{2,1,0:T(8,128)}, f32[4,16,128]{2,1,0:T(8,128)}), (f32[4,16,128]{2,1,0:T(8,128)}, f32[4,16,128]{2,1,0:T(8,128)})) %all-reduce.7.cloned.1.call-update) | async-done | bytes 65552 | tf_op jit(solution)/shard_map/psum | solution.py:139
  117.3 1.3 collective-permute-start
  118.6 4.5 %collective-permute-start.1 = (f32[4,1,128]{2,1,0:T(1,128)S(1)}, f32[4,1,128]{2,1,0:T(1,128)S(1)}, u32[]{:S(2)}, u32[]{:S(2)}) collective-permute-start(f32[4,1,128]{2,1,0:T(1,128)S(1)} %get-tuple-element.20), channel_id=1, source_target_pairs={{0,4},{4,8},{8,12},{1,5},{5,9},{9,13},{2,6},{6,10},{10,14},{3,7},{... | collective-permute-start | bytes 6152 | tf_op jit(solution)/shard_map/ppermute | solution.py:20
  123.1 1.3 collective-permute-done.1
  124.5 1.3 collective-permute-start.2
  125.8 4.5 %collective-permute-start.3 = (f32[4,18,1]{2,1,0:T(8,128)S(1)}, f32[4,18,1]{2,1,0:T(8,128)S(1)}, u32[]{:S(2)}, u32[]{:S(2)}) collective-permute-start(f32[4,18,1]{2,1,0:T(8,128)S(1)} %get-tuple-element.13), channel_id=1, source_target_pairs={{0,1},{1,2},{2,3},{4,5},{5,6},{6,7},{8,9},{9,10},{10,11},{12,13},{... | collective-permute-start | bytes 872 | tf_op jit(solution)/shard_map/ppermute | solution.py:20
  130.5 1.6 collective-permute-done.3
  132.2 1.3 collective-permute-start.4
  133.5 5.2 %collective-permute-start.5 = (f32[4,1,128]{2,1,0:T(1,128)S(1)}, f32[4,1,128]{2,1,0:T(1,128)S(1)}, u32[]{:S(2)}, u32[]{:S(2)}) collective-permute-start(f32[4,1,128]{2,1,0:T(1,128)S(1)} %get-tuple-element.18), channel_id=1, source_target_pairs={{0,4},{4,8},{8,12},{1,5},{5,9},{9,13},{2,6},{6,10},{10,14},{3,7},{... | collective-permute-start | bytes 6152 | tf_op jit(solution)/shard_map/ppermute | solution.py:20
  138.7 1.3 collective-permute-done.5
  140.1 1.3 collective-permute-start.6
  141.4 4.9 %collective-permute-start.7 = (f32[4,18,1]{2,1,0:T(8,128)S(1)}, f32[4,18,1]{2,1,0:T(8,128)S(1)}, u32[]{:S(2)}, u32[]{:S(2)}) collective-permute-start(f32[4,18,1]{2,1,0:T(8,128)S(1)} %get-tuple-element.11), channel_id=1, source_target_pairs={{0,1},{1,2},{2,3},{4,5},{5,6},{6,7},{8,9},{9,10},{10,11},{12,13},{... | collective-permute-start | bytes 872 | tf_op jit(solution)/shard_map/ppermute | solution.py:20
  146.4 1.6 collective-permute-done.7
  148.1 1.3 collective-permute-start.8
  149.4 5.7 %collective-permute-start.9 = (f32[4,1,128]{2,1,0:T(1,128)S(1)}, f32[4,1,128]{2,1,0:T(1,128)S(1)}, u32[]{:S(2)}, u32[]{:S(2)}) collective-permute-start(f32[4,1,128]{2,1,0:T(1,128)S(1)} %get-tuple-element.16), channel_id=1, source_target_pairs={{0,4},{4,8},{8,12},{1,5},{5,9},{9,13},{2,6},{6,10},{10,14},{3,7},{... | collective-permute-start | bytes 6152 | tf_op jit(solution)/shard_map/ppermute | solution.py:20
  155.1 1.3 collective-permute-done.9
  156.5 1.3 collective-permute-start.10
  157.8 4.9 %collective-permute-start.11 = (f32[4,18,1]{2,1,0:T(8,128)S(1)}, f32[4,18,1]{2,1,0:T(8,128)S(1)}, u32[]{:S(2)}, u32[]{:S(2)}) collective-permute-start(f32[4,18,1]{2,1,0:T(8,128)S(1)} %get-tuple-element.9), channel_id=1, source_target_pairs={{0,1},{1,2},{2,3},{4,5},{5,6},{6,7},{8,9},{9,10},{10,11},{12,13},{... | collective-permute-start | bytes 872 | tf_op jit(solution)/shard_map/ppermute | solution.py:20
  162.8 1.6 collective-permute-done.11
  164.6 1.3 collective-permute-start.12
  165.9 5.7 %collective-permute-start.13 = (f32[4,1,128]{2,1,0:T(1,128)S(1)}, f32[4,1,128]{2,1,0:T(1,128)S(1)}, u32[]{:S(2)}, u32[]{:S(2)}) collective-permute-start(f32[4,1,128]{2,1,0:T(1,128)S(1)} %get-tuple-element.14), channel_id=1, source_target_pairs={{0,4},{4,8},{8,12},{1,5},{5,9},{9,13},{2,6},{6,10},{10,14},{3,7},{... | collective-permute-start | bytes 6152 | tf_op jit(solution)/shard_map/ppermute | solution.py:20
  171.6 1.3 collective-permute-done.13
  172.9 1.3 collective-permute-start.14
  174.2 4.9 %collective-permute-start.15 = (f32[4,18,1]{2,1,0:T(8,128)S(1)}, f32[4,18,1]{2,1,0:T(8,128)S(1)}, u32[]{:S(2)}, u32[]{:S(2)}) collective-permute-start(f32[4,18,1]{2,1,0:T(8,128)S(1)} %get-tuple-element.7), channel_id=1, source_target_pairs={{0,1},{1,2},{2,3},{4,5},{5,6},{6,7},{8,9},{9,10},{10,11},{12,13},{... | collective-permute-start | bytes 872 | tf_op jit(solution)/shard_map/ppermute | solution.py:20
  179.3 1.6 collective-permute-done.15
  182.4 14.3 %all_to_all.41 = bf16[4,4,20,4,2,128]{5,4,3,2,1,0:T(2,128)(2,1)S(1)} all-to-all(bf16[4,4,20,4,2,128]{5,4,3,2,1,0:T(2,128)(2,1)S(1)} %reshape_reshape.11), channel_id=1, replica_groups=mesh['group'=2,'gx'=4,'gy'=4] {'gx'}, dimensions={0} | all-to-all | bytes 1310720 | tf_op jit(solution)/shard_map/all_to_all | solution.py:66
  196.8 1.3 copy.64
  198.1 6.8 %all-to-all-start.7 = ((bf16[4,4,20,4,2,128]{5,4,3,2,0,1:T(2,128)(2,1)}), bf16[4,4,20,4,2,128]{5,4,3,2,0,1:T(2,128)(2,1)S(1)}, u32[]{:S(2)}, u32[]{:S(2)}) async-start(bf16[4,4,20,4,2,128]{5,4,3,2,0,1:T(2,128)(2,1)} %copy.64), calls=%async_computation.7 | async-start | bytes 1310720 | tf_op jit(solution)/shard_map/all_to_all | solution.py:65
  205.0 11.7 %all-to-all-done.7 = bf16[4,4,20,4,2,128]{5,4,3,2,0,1:T(2,128)(2,1)S(1)} async-done(((bf16[4,4,20,4,2,128]{5,4,3,2,0,1:T(2,128)(2,1)}), bf16[4,4,20,4,2,128]{5,4,3,2,0,1:T(2,128)(2,1)S(1)}, u32[]{:S(2)}, u32[]{:S(2)}) %all-to-all-start.7) | async-done | bytes 655392 | tf_op jit(solution)/shard_map/all_to_all | solution.py:65
  217.1 1.7 gather_fusion
  218.9 1.7 broadcast_select_fusion
  (66 shorter events, 12.8 us)
Async XLA Ops:
  22.0 14.9 %all-to-all-start.1 = ((s32[4,4,20]{2,0,1:T(4,128)}), s32[4,4,20]{2,0,1:T(4,128)S(1)}, u32[]{:S(2)}, u32[]{:S(2)}) async-start(s32[4,4,20]{2,0,1:T(4,128)} %copy.49), calls=%async_computation.1 | async-start | bytes 16384 | tf_op jit(solution)/shard_map/all_to_all | solution.py:48
  36.9 3.6 %copy-start = (bf16[1,1,1,256,4,2,128]{6,5,4,3,2,1,0:T(2,128)(2,1)S(1)}, bf16[1,1,1,256,4,2,128]{6,5,4,3,2,1,0:T(2,128)(2,1)}, u32[]{:S(2)}) copy-start(bf16[1,1,1,256,4,2,128]{6,5,4,3,2,1,0:T(2,128)(2,1)} %param.5) | copy-start | bytes 1572868
  36.9 12.6 %all-to-all-start.4 = ((bf16[4,4,20,4,2,128]{5,4,3,2,1,0:T(2,128)(2,1)}), bf16[4,4,20,4,2,128]{5,4,3,2,1,0:T(2,128)(2,1)S(1)}, u32[]{:S(2)}, u32[]{:S(2)}) async-start(bf16[4,4,20,4,2,128]{5,4,3,2,1,0:T(2,128)(2,1)} %copy.58), calls=%async_computation.4 | async-start | bytes 1310720 | tf_op jit(solution)/shard_map/all_to_all | solution.py:42
  49.5 11.6 %all-to-all-start.2 = ((bf16[4,4,20,4,2,128]{5,4,3,2,1,0:T(2,128)(2,1)}), bf16[4,4,20,4,2,128]{5,4,3,2,1,0:T(2,128)(2,1)S(1)}, u32[]{:S(2)}, u32[]{:S(2)}) async-start(bf16[4,4,20,4,2,128]{5,4,3,2,1,0:T(2,128)(2,1)} %copy.52), calls=%async_computation.2 | async-start | bytes 1310720 | tf_op jit(solution)/shard_map/all_to_all | solution.py:35
  61.1 18.5 %all-to-all-start.5 = ((bf16[4,4,20,4,2,128]{5,4,3,2,0,1:T(2,128)(2,1)}), bf16[4,4,20,4,2,128]{5,4,3,2,0,1:T(2,128)(2,1)S(1)}, u32[]{:S(2)}, u32[]{:S(2)}) async-start(bf16[4,4,20,4,2,128]{5,4,3,2,0,1:T(2,128)(2,1)} %copy.59), calls=%async_computation.5 | async-start | bytes 1310720 | tf_op jit(solution)/shard_map/all_to_all | solution.py:41
  79.7 18.2 %all-to-all-start.3 = ((bf16[4,4,20,4,2,128]{5,4,3,2,0,1:T(2,128)(2,1)}), bf16[4,4,20,4,2,128]{5,4,3,2,0,1:T(2,128)(2,1)S(1)}, u32[]{:S(2)}, u32[]{:S(2)}) async-start(bf16[4,4,20,4,2,128]{5,4,3,2,0,1:T(2,128)(2,1)} %copy.53), calls=%async_computation.3 | async-start | bytes 1310720 | tf_op jit(solution)/shard_map/all_to_all | solution.py:34
  83.2 33.3 %all-reduce.7.cloned.1.call-start = ((), (), s32[]{:S(2)}) async-start(), calls=%async_computation.8 | async-start | bytes 131072 | tf_op jit(solution)/shard_map/psum | solution.py:139
  117.3 5.9 %collective-permute-start = (f32[4,1,128]{2,1,0:T(1,128)S(1)}, f32[4,1,128]{2,1,0:T(1,128)S(1)}, u32[]{:S(2)}, u32[]{:S(2)}) collective-permute-start(f32[4,1,128]{2,1,0:T(1,128)S(1)} %get-tuple-element.21), channel_id=1, source_target_pairs={{4,0},{8,4},{12,8},{5,1},{9,5},{13,9},{6,2},{10,6},{14,10},{7,3},{... | collective-permute-start | bytes 6152 | tf_op jit(solution)/shard_map/ppermute | solution.py:22
  118.6 5.8 %collective-permute-start.1 = (f32[4,1,128]{2,1,0:T(1,128)S(1)}, f32[4,1,128]{2,1,0:T(1,128)S(1)}, u32[]{:S(2)}, u32[]{:S(2)}) collective-permute-start(f32[4,1,128]{2,1,0:T(1,128)S(1)} %get-tuple-element.20), channel_id=1, source_target_pairs={{0,4},{4,8},{8,12},{1,5},{5,9},{9,13},{2,6},{6,10},{10,14},{3,7},{... | collective-permute-start | bytes 6152 | tf_op jit(solution)/shard_map/ppermute | solution.py:20
  124.5 6.0 %collective-permute-start.2 = (f32[4,18,1]{2,1,0:T(8,128)S(1)}, f32[4,18,1]{2,1,0:T(8,128)S(1)}, u32[]{:S(2)}, u32[]{:S(2)}) collective-permute-start(f32[4,18,1]{2,1,0:T(8,128)S(1)} %get-tuple-element.12), channel_id=1, source_target_pairs={{1,0},{2,1},{3,2},{5,4},{6,5},{7,6},{9,8},{10,9},{11,10},{13,12},{... | collective-permute-start | bytes 872 | tf_op jit(solution)/shard_map/ppermute | solution.py:22
  125.8 6.3 %collective-permute-start.3 = (f32[4,18,1]{2,1,0:T(8,128)S(1)}, f32[4,18,1]{2,1,0:T(8,128)S(1)}, u32[]{:S(2)}, u32[]{:S(2)}) collective-permute-start(f32[4,18,1]{2,1,0:T(8,128)S(1)} %get-tuple-element.13), channel_id=1, source_target_pairs={{0,1},{1,2},{2,3},{4,5},{5,6},{6,7},{8,9},{9,10},{10,11},{12,13},{... | collective-permute-start | bytes 872 | tf_op jit(solution)/shard_map/ppermute | solution.py:20
  132.2 48.7 %copy-start.1 = (f32[4,16,128]{2,1,0:T(8,128)S(1)}, f32[4,16,128]{2,1,0:T(8,128)}, u32[]{:S(2)}) copy-start(f32[4,16,128]{2,1,0:T(8,128)} %param.9) | copy-start | bytes 98308
  132.2 6.5 %collective-permute-start.4 = (f32[4,1,128]{2,1,0:T(1,128)S(1)}, f32[4,1,128]{2,1,0:T(1,128)S(1)}, u32[]{:S(2)}, u32[]{:S(2)}) collective-permute-start(f32[4,1,128]{2,1,0:T(1,128)S(1)} %get-tuple-element.19), channel_id=1, source_target_pairs={{4,0},{8,4},{12,8},{5,1},{9,5},{13,9},{6,2},{10,6},{14,10},{7,3},{... | collective-permute-start | bytes 6152 | tf_op jit(solution)/shard_map/ppermute | solution.py:22
  133.5 6.5 %collective-permute-start.5 = (f32[4,1,128]{2,1,0:T(1,128)S(1)}, f32[4,1,128]{2,1,0:T(1,128)S(1)}, u32[]{:S(2)}, u32[]{:S(2)}) collective-permute-start(f32[4,1,128]{2,1,0:T(1,128)S(1)} %get-tuple-element.18), channel_id=1, source_target_pairs={{0,4},{4,8},{8,12},{1,5},{5,9},{9,13},{2,6},{6,10},{10,14},{3,7},{... | collective-permute-start | bytes 6152 | tf_op jit(solution)/shard_map/ppermute | solution.py:20
  140.1 6.3 %collective-permute-start.6 = (f32[4,18,1]{2,1,0:T(8,128)S(1)}, f32[4,18,1]{2,1,0:T(8,128)S(1)}, u32[]{:S(2)}, u32[]{:S(2)}) collective-permute-start(f32[4,18,1]{2,1,0:T(8,128)S(1)} %get-tuple-element.10), channel_id=1, source_target_pairs={{1,0},{2,1},{3,2},{5,4},{6,5},{7,6},{9,8},{10,9},{11,10},{13,12},{... | collective-permute-start | bytes 872 | tf_op jit(solution)/shard_map/ppermute | solution.py:22
  141.4 6.6 %collective-permute-start.7 = (f32[4,18,1]{2,1,0:T(8,128)S(1)}, f32[4,18,1]{2,1,0:T(8,128)S(1)}, u32[]{:S(2)}, u32[]{:S(2)}) collective-permute-start(f32[4,18,1]{2,1,0:T(8,128)S(1)} %get-tuple-element.11), channel_id=1, source_target_pairs={{0,1},{1,2},{2,3},{4,5},{5,6},{6,7},{8,9},{9,10},{10,11},{12,13},{... | collective-permute-start | bytes 872 | tf_op jit(solution)/shard_map/ppermute | solution.py:20
  148.1 7.0 %collective-permute-start.8 = (f32[4,1,128]{2,1,0:T(1,128)S(1)}, f32[4,1,128]{2,1,0:T(1,128)S(1)}, u32[]{:S(2)}, u32[]{:S(2)}) collective-permute-start(f32[4,1,128]{2,1,0:T(1,128)S(1)} %get-tuple-element.17), channel_id=1, source_target_pairs={{4,0},{8,4},{12,8},{5,1},{9,5},{13,9},{6,2},{10,6},{14,10},{7,3},{... | collective-permute-start | bytes 6152 | tf_op jit(solution)/shard_map/ppermute | solution.py:22
  149.4 7.0 %collective-permute-start.9 = (f32[4,1,128]{2,1,0:T(1,128)S(1)}, f32[4,1,128]{2,1,0:T(1,128)S(1)}, u32[]{:S(2)}, u32[]{:S(2)}) collective-permute-start(f32[4,1,128]{2,1,0:T(1,128)S(1)} %get-tuple-element.16), channel_id=1, source_target_pairs={{0,4},{4,8},{8,12},{1,5},{5,9},{9,13},{2,6},{6,10},{10,14},{3,7},{... | collective-permute-start | bytes 6152 | tf_op jit(solution)/shard_map/ppermute | solution.py:20
  156.5 6.3 %collective-permute-start.10 = (f32[4,18,1]{2,1,0:T(8,128)S(1)}, f32[4,18,1]{2,1,0:T(8,128)S(1)}, u32[]{:S(2)}, u32[]{:S(2)}) collective-permute-start(f32[4,18,1]{2,1,0:T(8,128)S(1)} %get-tuple-element.8), channel_id=1, source_target_pairs={{1,0},{2,1},{3,2},{5,4},{6,5},{7,6},{9,8},{10,9},{11,10},{13,12},{... | collective-permute-start | bytes 872 | tf_op jit(solution)/shard_map/ppermute | solution.py:22
  157.8 6.6 %collective-permute-start.11 = (f32[4,18,1]{2,1,0:T(8,128)S(1)}, f32[4,18,1]{2,1,0:T(8,128)S(1)}, u32[]{:S(2)}, u32[]{:S(2)}) collective-permute-start(f32[4,18,1]{2,1,0:T(8,128)S(1)} %get-tuple-element.9), channel_id=1, source_target_pairs={{0,1},{1,2},{2,3},{4,5},{5,6},{6,7},{8,9},{9,10},{10,11},{12,13},{... | collective-permute-start | bytes 872 | tf_op jit(solution)/shard_map/ppermute | solution.py:20
  164.6 7.0 %collective-permute-start.12 = (f32[4,1,128]{2,1,0:T(1,128)S(1)}, f32[4,1,128]{2,1,0:T(1,128)S(1)}, u32[]{:S(2)}, u32[]{:S(2)}) collective-permute-start(f32[4,1,128]{2,1,0:T(1,128)S(1)} %get-tuple-element.15), channel_id=1, source_target_pairs={{4,0},{8,4},{12,8},{5,1},{9,5},{13,9},{6,2},{10,6},{14,10},{7,3},{... | collective-permute-start | bytes 6152 | tf_op jit(solution)/shard_map/ppermute | solution.py:22
  165.9 7.0 %collective-permute-start.13 = (f32[4,1,128]{2,1,0:T(1,128)S(1)}, f32[4,1,128]{2,1,0:T(1,128)S(1)}, u32[]{:S(2)}, u32[]{:S(2)}) collective-permute-start(f32[4,1,128]{2,1,0:T(1,128)S(1)} %get-tuple-element.14), channel_id=1, source_target_pairs={{0,4},{4,8},{8,12},{1,5},{5,9},{9,13},{2,6},{6,10},{10,14},{3,7},{... | collective-permute-start | bytes 6152 | tf_op jit(solution)/shard_map/ppermute | solution.py:20
  172.9 6.3 %collective-permute-start.14 = (f32[4,18,1]{2,1,0:T(8,128)S(1)}, f32[4,18,1]{2,1,0:T(8,128)S(1)}, u32[]{:S(2)}, u32[]{:S(2)}) collective-permute-start(f32[4,18,1]{2,1,0:T(8,128)S(1)} %get-tuple-element.6), channel_id=1, source_target_pairs={{1,0},{2,1},{3,2},{5,4},{6,5},{7,6},{9,8},{10,9},{11,10},{13,12},{... | collective-permute-start | bytes 872 | tf_op jit(solution)/shard_map/ppermute | solution.py:22
  174.2 6.6 %collective-permute-start.15 = (f32[4,18,1]{2,1,0:T(8,128)S(1)}, f32[4,18,1]{2,1,0:T(8,128)S(1)}, u32[]{:S(2)}, u32[]{:S(2)}) collective-permute-start(f32[4,18,1]{2,1,0:T(8,128)S(1)} %get-tuple-element.7), channel_id=1, source_target_pairs={{0,1},{1,2},{2,3},{4,5},{5,6},{6,7},{8,9},{9,10},{10,11},{12,13},{... | collective-permute-start | bytes 872 | tf_op jit(solution)/shard_map/ppermute | solution.py:20
  198.1 6.8 %copy-start.2 = (s32[1,1,1,256]{3,2,1,0:T(1,128)S(1)}, s32[1,1,1,256]{3,2,1,0:T(1,128)}, u32[]{:S(2)}) copy-start(s32[1,1,1,256]{3,2,1,0:T(1,128)} %param.7) | copy-start | bytes 3076
  198.1 18.5 %all-to-all-start.7 = ((bf16[4,4,20,4,2,128]{5,4,3,2,0,1:T(2,128)(2,1)}), bf16[4,4,20,4,2,128]{5,4,3,2,0,1:T(2,128)(2,1)S(1)}, u32[]{:S(2)}, u32[]{:S(2)}) async-start(bf16[4,4,20,4,2,128]{5,4,3,2,0,1:T(2,128)(2,1)} %copy.64), calls=%async_computation.7 | async-start | bytes 1310720 | tf_op jit(solution)/shard_map/all_to_all | solution.py:65
Sparse Core Ops, SparseCore 0:
  100.2 16.1 all-reduce.6
where the time goes:
time: 229 us; the launch traced here: 227 us
  starting transfers between devices  78.5 us (34%)
  waiting for transfers between devices  70.8 us (31%)
  local copies, waits for them, and re-layouts  32.6 us (14%)
  blocking collectives  24 us (10%)
  between operations  14.4 us (6%)
  other arithmetic  6.4 us (3%)
    ppermute x8, starting transfers between devices, with_halo(): lax.ppermute(tail, axis, [(i, (i + 1) % count) for i in range(ends)])  40.3 us
    psum x1, waiting for transfers between devices, local(): lax.psum((to_tile(grad_sum), to_tile(illum_sum)), 'group')  16.3 us
    all_to_all x1, blocking collectives, send_back(): lax.all_to_all(sectioned_back, 'gx', split_axis=0, concat_axis=0, tiled=T...  14.3 us
    all_to_all x1, waiting for transfers between devices, deliver(): lax.all_to_all(lax.all_to_all(sectioned_grad, 'gx', split_axis=0, concat_...  12.3 us
    all_to_all x1, waiting for transfers between devices, deliver(): lax.all_to_all(lax.all_to_all(sectioned_illum, 'gx', split_axis=0, concat...  12.3 us
    all_to_all x1, waiting for transfers between devices, send_back(): lax.all_to_all(lax.all_to_all(sectioned_back, 'gx', split_axis=0, concat_...  11.7 us
    ppermute x8, waiting for transfers between devices, with_halo(): lax.ppermute(tail, axis, [(i, (i + 1) % count) for i in range(ends)])  11.5 us
    ppermute x8, starting transfers between devices, with_halo(): lax.ppermute(head, axis, [((i + 1) % count, i) for i in range(ends)])  10.3 us
  transfers between devices with their start and end apart: 23, of which 17 were waited for; matrix products, arithmetic and copies ran while one was open for 11% of the time, Pallas kernels for 0%

commit v1 on v0

--- a/solution.py
+++ b/solution.py
@@ -7,6 +7,29 @@
 damping = 10.0
 smooth_rate = 0.12
 step_length = 24.0
+
+
+def cut_along(shard, dim, peers):
+    shape = shard.shape
+    tiles = shard.reshape(*shape[:dim], peers, shape[dim] // peers, *shape[dim + 1 :])
+    return jnp.moveaxis(tiles, dim, 0)
+
+
+def laid_out(blocks, dim):
+    dims = list(blocks.shape[1:])
+    dims[dim] *= blocks.shape[0]
+    return jnp.moveaxis(blocks, 0, dim).reshape(dims)
+
+
+def pairwise_exchange(array, axis, split_dim, concat_dim):
+    size, index = (lax.axis_size(axis), lax.axis_index(axis))
+    pieces = cut_along(array, split_dim, size)
+    outs = [pieces[index]]
+    for lap in range(1, size):
+        sent = pieces[index ^ lap]
+        outs.append(lax.ppermute(sent, axis, [(i, i ^ lap) for i in range(size)]))
+    pieces = jnp.stack(outs)[index ^ jnp.arange(size)]
+    return laid_out(pieces, concat_dim)
 
 
 def with_halo(cells, sides, width):
@@ -45,12 +68,11 @@
             concat_axis=1,
             tiled=True,
         ),
-        lax.all_to_all(
+        pairwise_exchange(
             lax.all_to_all(sectioned_patch, "gx", split_axis=0, concat_axis=0, tiled=True),
             "gy",
-            split_axis=1,
-            concat_axis=1,
-            tiled=True,
+            1,
+            1,
         ),
     )
     return (

time: 229 us -> 227 us (level)
  blocking collectives: 24 us -> 14.3 us
  waiting for transfers between devices: 70.8 us -> 74.7 us
  starting transfers between devices: 78.5 us -> 82.3 us
    all_to_all x1, waiting for transfers between devices: 12.3 us -> 0.01 us  [deliver(): lax.all_to_all(lax.all_to_all(sectioned_grad, 'gx', split_axis=0, concat_...]
    ppermute x0 -> x3, waiting for transfers between devices: none -> 11.8 us  [pairwise_exchange(): outs.append(lax.ppermute(sent, axis, [(i, i ^ lap) for i in range(size)]))]
    all_to_all x1 -> x0, blocking collectives: 9.66 us -> none  [deliver(): lax.all_to_all(sectioned_patch, 'gx', split_axis=0, concat_axis=0, tiled=...]
    ppermute x0 -> x3, starting transfers between devices: none -> 4.45 us  [pairwise_exchange(): outs.append(lax.ppermute(sent, axis, [(i, i ^ lap) for i in range(size)]))]
    ppermute x8, waiting for transfers between devices: 0.52 us -> 4.64 us  [with_halo(): lax.ppermute(head, axis, [((i + 1) % count, i) for i in range(ends)])]
  transfers between devices with their start and end apart: 23 -> 26, of which waited for: 17 -> 18; matrix products, arithmetic and copies ran while one was open for 11% -> 11% of each run, Pallas kernels for 0% -> 0%
where the time goes in v1:
time: 227 us; the launch traced here: 226 us
  starting transfers between devices  82.3 us (36%)
  waiting for transfers between devices  74.7 us (33%)
  local copies, waits for them, and re-layouts  33.1 us (15%)
  between operations  14.4 us (6%)
  blocking collectives  14.3 us (6%)
  other arithmetic  6.41 us (3%)
    ppermute x8, starting transfers between devices, with_halo(): lax.ppermute(tail, axis, [(i, (i + 1) % count) for i in range(ends)])  39.3 us
    psum x1, waiting for transfers between devices, local(): lax.psum((to_tile(grad_sum), to_tile(illum_sum)), 'group')  15.1 us
    all_to_all x1, blocking collectives, send_back(): lax.all_to_all(sectioned_back, 'gx', split_axis=0, concat_axis=0, tiled=T...  14.3 us
    all_to_all x1, waiting for transfers between devices, deliver(): lax.all_to_all(lax.all_to_all(sectioned_illum, 'gx', split_axis=0, concat...  14.1 us
    ppermute x3, waiting for transfers between devices, pairwise_exchange(): outs.append(lax.ppermute(sent, axis, [(i, i ^ lap) for i in range(size)]))  11.8 us
    all_to_all x1, waiting for transfers between devices, send_back(): lax.all_to_all(lax.all_to_all(sectioned_back, 'gx', split_axis=0, concat_...  11.7 us
    ppermute x8, waiting for transfers between devices, with_halo(): lax.ppermute(tail, axis, [(i, (i + 1) % count) for i in range(ends)])  10.4 us
    ppermute x8, starting transfers between devices, with_halo(): lax.ppermute(head, axis, [((i + 1) % count, i) for i in range(ends)])  10.3 us
  transfers between devices with their start and end apart: 26, of which 18 were waited for; matrix products, arithmetic and copies ran while one was open for 11% of the time, Pallas kernels for 0%

profile of v1, /device:TPU:0, one launch (start us, length us, event | category | flops | bytes accessed | tf_op | source)
XLA Modules:
  0.0 226.1 jit_solution(12489800730515829734)
XLA Ops:
  10.1 1.6 scatter_custom_fusion
  12.4 5.2 %all-to-all-start = ((s32[4,4,20]{2,1,0:T(4,128)}), s32[4,4,20]{2,1,0:T(4,128)S(1)}, u32[]{:S(2)}, u32[]{:S(2)}) async-start(s32[4,4,20]{2,1,0:T(4,128)} %reshape.129), calls=%async_computation | async-start | bytes 16384 | tf_op jit(solution)/shard_map/all_to_all | solution.py:72
  18.9 7.1 %scatter_fusion.1 = bf16[320,4,2,128]{3,1,2,0:T(4,128)(2,1)S(1)} fusion(bf16[320,4,2,128]{3,1,2,0:T(4,128)(2,1)S(1)} %broadcast.138.clone.1, s32[256]{0:T(256)S(1)} %bitcast.83, bf16[256,4,2,128]{3,1,2,0:T(4,128)(2,1)S(1)} %copy.57), kind=kCustom, calls=%fused_computation.4 | custom fusion | bytes 1573888 | tf_op jit(solution)/shard_map/scatter | solution.py:138
  26.0 1.5 copy.58
  27.5 4.3 %all-to-all-start.3 = ((bf16[4,4,20,4,2,128]{5,4,3,2,1,0:T(2,128)(2,1)}), bf16[4,4,20,4,2,128]{5,4,3,2,1,0:T(2,128)(2,1)S(1)}, u32[]{:S(2)}, u32[]{:S(2)}) async-start(bf16[4,4,20,4,2,128]{5,4,3,2,1,0:T(2,128)(2,1)} %copy.58), calls=%async_computation.3 | async-start | bytes 1310720 | tf_op jit(solution)/shard_map/all_to_all | solution.py:65
  32.2 7.1 %scatter_fusion = bf16[320,4,2,128]{3,1,2,0:T(4,128)(2,1)S(1)} fusion(bf16[320,4,2,128]{3,1,2,0:T(4,128)(2,1)S(1)} %broadcast.138.clone, s32[256]{0:T(256)S(1)} %bitcast.84, bf16[256,4,2,128]{3,1,2,0:T(4,128)(2,1)S(1)} %copy.51), kind=kCustom, calls=%fused_computation.3 | custom fusion | bytes 1573888 | tf_op jit(solution)/shard_map/scatter | solution.py:133
  39.3 1.5 copy.52
  40.8 4.2 %all-to-all-start.1 = ((bf16[4,4,20,4,2,128]{5,4,3,2,1,0:T(2,128)(2,1)}), bf16[4,4,20,4,2,128]{5,4,3,2,1,0:T(2,128)(2,1)S(1)}, u32[]{:S(2)}, u32[]{:S(2)}) async-start(bf16[4,4,20,4,2,128]{5,4,3,2,1,0:T(2,128)(2,1)} %copy.52), calls=%async_computation.1 | async-start | bytes 1310720 | tf_op jit(solution)/shard_map/all_to_all | solution.py:58
  45.0 1.3 copy.59
  46.4 7.0 %all-to-all-done.1 = bf16[4,4,20,4,2,128]{5,4,3,2,1,0:T(2,128)(2,1)S(1)} async-done(((bf16[4,4,20,4,2,128]{5,4,3,2,1,0:T(2,128)(2,1)}), bf16[4,4,20,4,2,128]{5,4,3,2,1,0:T(2,128)(2,1)S(1)}, u32[]{:S(2)}, u32[]{:S(2)}) %all-to-all-start.1) | async-done | bytes 655392 | tf_op jit(solution)/shard_map/all_to_all | solution.py:58
  53.3 4.9 %all-to-all-start.4 = ((bf16[4,4,20,4,2,128]{5,4,3,2,0,1:T(2,128)(2,1)}), bf16[4,4,20,4,2,128]{5,4,3,2,0,1:T(2,128)(2,1)S(1)}, u32[]{:S(2)}, u32[]{:S(2)}) async-start(bf16[4,4,20,4,2,128]{5,4,3,2,0,1:T(2,128)(2,1)} %copy.59), calls=%async_computation.4 | async-start | bytes 1310720 | tf_op jit(solution)/shard_map/all_to_all | solution.py:64
  58.2 1.3 copy.53
  59.5 14.1 %all-to-all-done.4 = bf16[4,4,20,4,2,128]{5,4,3,2,0,1:T(2,128)(2,1)S(1)} async-done(((bf16[4,4,20,4,2,128]{5,4,3,2,0,1:T(2,128)(2,1)}), bf16[4,4,20,4,2,128]{5,4,3,2,0,1:T(2,128)(2,1)S(1)}, u32[]{:S(2)}, u32[]{:S(2)}) %all-to-all-start.4) | async-done | bytes 655392 | tf_op jit(solution)/shard_map/all_to_all | solution.py:64
  73.6 3.5 %all-to-all-start.2 = ((bf16[4,4,20,4,2,128]{5,4,3,2,0,1:T(2,128)(2,1)}), bf16[4,4,20,4,2,128]{5,4,3,2,0,1:T(2,128)(2,1)S(1)}, u32[]{:S(2)}, u32[]{:S(2)}) async-start(bf16[4,4,20,4,2,128]{5,4,3,2,0,1:T(2,128)(2,1)} %copy.53), calls=%async_computation.2 | async-start | bytes 1310720 | tf_op jit(solution)/shard_map/all_to_all | solution.py:57
  77.2 3.8 %collective-permute-start.2 = (s32[4,1,20]{2,1,0:T(1,128)S(1)}, s32[4,1,20]{2,1,0:T(1,128)S(1)}, u32[]{:S(2)}, u32[]{:S(2)}) collective-permute-start(s32[4,1,20]{2,1,0:T(1,128)S(1)} %get-tuple-element.23), channel_id=1, source_target_pairs={{0,3},{1,2},{2,1},{3,0},{4,7},{5,6},{6,5},{7,4},{8,11},{9,10},{10,... | collective-permute-start | bytes 968 | tf_op jit(solution)/shard_map/ppermute | solution.py:30
  81.7 9.3 %collective-permute-done.2 = s32[4,1,20]{2,1,0:T(1,128)S(1)} collective-permute-done((s32[4,1,20]{2,1,0:T(1,128)S(1)}, s32[4,1,20]{2,1,0:T(1,128)S(1)}, u32[]{:S(2)}, u32[]{:S(2)}) %collective-permute-start.2) | collective-permute-done | bytes 352 | tf_op jit(solution)/shard_map/ppermute | solution.py:30
  91.0 2.5 %collective-permute-done.1 = s32[4,1,20]{2,1,0:T(1,128)S(1)} collective-permute-done((s32[4,1,20]{2,1,0:T(1,128)S(1)}, s32[4,1,20]{2,1,0:T(1,128)S(1)}, u32[]{:S(2)}, u32[]{:S(2)}) %collective-permute-start.1) | collective-permute-done | bytes 352 | tf_op jit(solution)/shard_map/ppermute | solution.py:30
  98.7 15.1 %all-reduce.7.cloned.1.call-done = (f32[4,16,128]{2,1,0:T(8,128)}, f32[4,16,128]{2,1,0:T(8,128)}) async-done(((f32[4,16,128]{2,1,0:T(8,128)}, f32[4,16,128]{2,1,0:T(8,128)}), (f32[4,16,128]{2,1,0:T(8,128)}, f32[4,16,128]{2,1,0:T(8,128)})) %all-reduce.7.cloned.1.call-update) | async-done | bytes 65552 | tf_op jit(solution)/shard_map/psum | solution.py:161
  114.6 1.3 collective-permute-start.3
  115.9 4.5 %collective-permute-start.4 = (f32[4,1,128]{2,1,0:T(1,128)S(1)}, f32[4,1,128]{2,1,0:T(1,128)S(1)}, u32[]{:S(2)}, u32[]{:S(2)}) collective-permute-start(f32[4,1,128]{2,1,0:T(1,128)S(1)} %get-tuple-element.20), channel_id=1, source_target_pairs={{0,4},{4,8},{8,12},{1,5},{5,9},{9,13},{2,6},{6,10},{10,14},{3,7},{... | collective-permute-start | bytes 6152 | tf_op jit(solution)/shard_map/ppermute | solution.py:43
  120.5 1.3 collective-permute-done.4
  121.9 1.3 collective-permute-start.5
  123.2 4.5 %collective-permute-start.6 = (f32[4,18,1]{2,1,0:T(8,128)S(1)}, f32[4,18,1]{2,1,0:T(8,128)S(1)}, u32[]{:S(2)}, u32[]{:S(2)}) collective-permute-start(f32[4,18,1]{2,1,0:T(8,128)S(1)} %get-tuple-element.13), channel_id=1, source_target_pairs={{0,1},{1,2},{2,3},{4,5},{5,6},{6,7},{8,9},{9,10},{10,11},{12,13},{... | collective-permute-start | bytes 872 | tf_op jit(solution)/shard_map/ppermute | solution.py:43
  127.8 1.6 collective-permute-done.6
  129.6 1.3 collective-permute-start.7
  130.9 5.2 %collective-permute-start.8 = (f32[4,1,128]{2,1,0:T(1,128)S(1)}, f32[4,1,128]{2,1,0:T(1,128)S(1)}, u32[]{:S(2)}, u32[]{:S(2)}) collective-permute-start(f32[4,1,128]{2,1,0:T(1,128)S(1)} %get-tuple-element.18), channel_id=1, source_target_pairs={{0,4},{4,8},{8,12},{1,5},{5,9},{9,13},{2,6},{6,10},{10,14},{3,7},{... | collective-permute-start | bytes 6152 | tf_op jit(solution)/shard_map/ppermute | solution.py:43
  136.1 1.3 collective-permute-done.8
  137.4 4.2 %collective-permute-start.10 = (f32[4,18,1]{2,1,0:T(8,128)S(1)}, f32[4,18,1]{2,1,0:T(8,128)S(1)}, u32[]{:S(2)}, u32[]{:S(2)}) collective-permute-start(f32[4,18,1]{2,1,0:T(8,128)S(1)} %get-tuple-element.11), channel_id=1, source_target_pairs={{0,1},{1,2},{2,3},{4,5},{5,6},{6,7},{8,9},{9,10},{10,11},{12,13},{... | collective-permute-start | bytes 872 | tf_op jit(solution)/shard_map/ppermute | solution.py:43
  141.7 1.3 collective-permute-start.9
  143.4 4.3 %collective-permute-done.9 = f32[4,18,1]{2,1,0:T(8,128)S(1)} collective-permute-done((f32[4,18,1]{2,1,0:T(8,128)S(1)}, f32[4,18,1]{2,1,0:T(8,128)S(1)}, u32[]{:S(2)}, u32[]{:S(2)}) %collective-permute-start.9) | collective-permute-done | bytes 320 | tf_op jit(solution)/shard_map/ppermute | solution.py:45
  147.8 1.3 collective-permute-start.11
  149.1 5.7 %collective-permute-start.12 = (f32[4,1,128]{2,1,0:T(1,128)S(1)}, f32[4,1,128]{2,1,0:T(1,128)S(1)}, u32[]{:S(2)}, u32[]{:S(2)}) collective-permute-start(f32[4,1,128]{2,1,0:T(1,128)S(1)} %get-tuple-element.16), channel_id=1, source_target_pairs={{0,4},{4,8},{8,12},{1,5},{5,9},{9,13},{2,6},{6,10},{10,14},{3,7},{... | collective-permute-start | bytes 6152 | tf_op jit(solution)/shard_map/ppermute | solution.py:43
  154.8 1.3 collective-permute-done.12
  156.2 1.3 collective-permute-start.13
  157.5 4.5 %collective-permute-start.14 = (f32[4,18,1]{2,1,0:T(8,128)S(1)}, f32[4,18,1]{2,1,0:T(8,128)S(1)}, u32[]{:S(2)}, u32[]{:S(2)}) collective-permute-start(f32[4,18,1]{2,1,0:T(8,128)S(1)} %get-tuple-element.9), channel_id=1, source_target_pairs={{0,1},{1,2},{2,3},{4,5},{5,6},{6,7},{8,9},{9,10},{10,11},{12,13},{... | collective-permute-start | bytes 872 | tf_op jit(solution)/shard_map/ppermute | solution.py:43
  162.2 1.6 collective-permute-done.14
  163.9 1.3 collective-permute-start.15
  165.2 5.7 %collective-permute-start.16 = (f32[4,1,128]{2,1,0:T(1,128)S(1)}, f32[4,1,128]{2,1,0:T(1,128)S(1)}, u32[]{:S(2)}, u32[]{:S(2)}) collective-permute-start(f32[4,1,128]{2,1,0:T(1,128)S(1)} %get-tuple-element.14), channel_id=1, source_target_pairs={{0,4},{4,8},{8,12},{1,5},{5,9},{9,13},{2,6},{6,10},{10,14},{3,7},{... | collective-permute-start | bytes 6152 | tf_op jit(solution)/shard_map/ppermute | solution.py:43
  170.9 1.3 collective-permute-done.16
  172.3 1.3 collective-permute-start.17
  173.6 4.9 %collective-permute-start.18 = (f32[4,18,1]{2,1,0:T(8,128)S(1)}, f32[4,18,1]{2,1,0:T(8,128)S(1)}, u32[]{:S(2)}, u32[]{:S(2)}) collective-permute-start(f32[4,18,1]{2,1,0:T(8,128)S(1)} %get-tuple-element.7), channel_id=1, source_target_pairs={{0,1},{1,2},{2,3},{4,5},{5,6},{6,7},{8,9},{9,10},{10,11},{12,13},{... | collective-permute-start | bytes 872 | tf_op jit(solution)/shard_map/ppermute | solution.py:43
  178.6 1.6 collective-permute-done.18
  181.8 14.3 %all_to_all.35 = bf16[4,4,20,4,2,128]{5,4,3,2,1,0:T(2,128)(2,1)S(1)} all-to-all(bf16[4,4,20,4,2,128]{5,4,3,2,1,0:T(2,128)(2,1)S(1)} %reshape_reshape.11), channel_id=1, replica_groups=mesh['group'=2,'gx'=4,'gy'=4] {'gx'}, dimensions={0} | all-to-all | bytes 1310720 | tf_op jit(solution)/shard_map/all_to_all | solution.py:88
  196.1 1.3 copy.64
  197.5 6.1 %all-to-all-start.6 = ((bf16[4,4,20,4,2,128]{5,4,3,2,0,1:T(2,128)(2,1)}), bf16[4,4,20,4,2,128]{5,4,3,2,0,1:T(2,128)(2,1)S(1)}, u32[]{:S(2)}, u32[]{:S(2)}) async-start(bf16[4,4,20,4,2,128]{5,4,3,2,0,1:T(2,128)(2,1)} %copy.64), calls=%async_computation.6 | async-start | bytes 1310720 | tf_op jit(solution)/shard_map/all_to_all | solution.py:87
  203.6 11.7 %all-to-all-done.6 = bf16[4,4,20,4,2,128]{5,4,3,2,0,1:T(2,128)(2,1)S(1)} async-done(((bf16[4,4,20,4,2,128]{5,4,3,2,0,1:T(2,128)(2,1)}), bf16[4,4,20,4,2,128]{5,4,3,2,0,1:T(2,128)(2,1)S(1)}, u32[]{:S(2)}, u32[]{:S(2)}) %all-to-all-start.6) | async-done | bytes 655392 | tf_op jit(solution)/shard_map/all_to_all | solution.py:87
  215.7 1.7 gather_fusion.1
  217.5 1.7 broadcast_select_fusion
  (75 shorter events, 15.7 us)
Async XLA Ops:
  12.4 15.2 %all-to-all-start = ((s32[4,4,20]{2,1,0:T(4,128)}), s32[4,4,20]{2,1,0:T(4,128)S(1)}, u32[]{:S(2)}, u32[]{:S(2)}) async-start(s32[4,4,20]{2,1,0:T(4,128)} %reshape.129), calls=%async_computation | async-start | bytes 16384 | tf_op jit(solution)/shard_map/all_to_all | solution.py:72
  27.5 4.3 %copy-start = (bf16[1,1,1,256,4,2,128]{6,5,4,3,2,1,0:T(2,128)(2,1)S(1)}, bf16[1,1,1,256,4,2,128]{6,5,4,3,2,1,0:T(2,128)(2,1)}, u32[]{:S(2)}) copy-start(bf16[1,1,1,256,4,2,128]{6,5,4,3,2,1,0:T(2,128)(2,1)} %param.5) | copy-start | bytes 1572868
  27.5 13.3 %all-to-all-start.3 = ((bf16[4,4,20,4,2,128]{5,4,3,2,1,0:T(2,128)(2,1)}), bf16[4,4,20,4,2,128]{5,4,3,2,1,0:T(2,128)(2,1)S(1)}, u32[]{:S(2)}, u32[]{:S(2)}) async-start(bf16[4,4,20,4,2,128]{5,4,3,2,1,0:T(2,128)(2,1)} %copy.58), calls=%async_computation.3 | async-start | bytes 1310720 | tf_op jit(solution)/shard_map/all_to_all | solution.py:65
  40.8 12.5 %all-to-all-start.1 = ((bf16[4,4,20,4,2,128]{5,4,3,2,1,0:T(2,128)(2,1)}), bf16[4,4,20,4,2,128]{5,4,3,2,1,0:T(2,128)(2,1)S(1)}, u32[]{:S(2)}, u32[]{:S(2)}) async-start(bf16[4,4,20,4,2,128]{5,4,3,2,1,0:T(2,128)(2,1)} %copy.52), calls=%async_computation.1 | async-start | bytes 1310720 | tf_op jit(solution)/shard_map/all_to_all | solution.py:58
  53.3 20.3 %all-to-all-start.4 = ((bf16[4,4,20,4,2,128]{5,4,3,2,0,1:T(2,128)(2,1)}), bf16[4,4,20,4,2,128]{5,4,3,2,0,1:T(2,128)(2,1)S(1)}, u32[]{:S(2)}, u32[]{:S(2)}) async-start(bf16[4,4,20,4,2,128]{5,4,3,2,0,1:T(2,128)(2,1)} %copy.59), calls=%async_computation.4 | async-start | bytes 1310720 | tf_op jit(solution)/shard_map/all_to_all | solution.py:64
  73.6 22.8 %all-to-all-start.2 = ((bf16[4,4,20,4,2,128]{5,4,3,2,0,1:T(2,128)(2,1)}), bf16[4,4,20,4,2,128]{5,4,3,2,0,1:T(2,128)(2,1)S(1)}, u32[]{:S(2)}, u32[]{:S(2)}) async-start(bf16[4,4,20,4,2,128]{5,4,3,2,0,1:T(2,128)(2,1)} %copy.53), calls=%async_computation.2 | async-start | bytes 1310720 | tf_op jit(solution)/shard_map/all_to_all | solution.py:57
  77.1 36.7 %all-reduce.7.cloned.1.call-start = ((), (), s32[]{:S(2)}) async-start(), calls=%async_computation.7 | async-start | bytes 131072 | tf_op jit(solution)/shard_map/psum | solution.py:161
  77.2 13.8 %collective-permute-start.2 = (s32[4,1,20]{2,1,0:T(1,128)S(1)}, s32[4,1,20]{2,1,0:T(1,128)S(1)}, u32[]{:S(2)}, u32[]{:S(2)}) collective-permute-start(s32[4,1,20]{2,1,0:T(1,128)S(1)} %get-tuple-element.23), channel_id=1, source_target_pairs={{0,3},{1,2},{2,1},{3,0},{4,7},{5,6},{6,5},{7,4},{8,11},{9,10},{10,... | collective-permute-start | bytes 968 | tf_op jit(solution)/shard_map/ppermute | solution.py:30
  81.0 10.0 %collective-permute-start = (s32[4,1,20]{2,1,0:T(1,128)S(1)}, s32[4,1,20]{2,1,0:T(1,128)S(1)}, u32[]{:S(2)}, u32[]{:S(2)}) collective-permute-start(s32[4,1,20]{2,1,0:T(1,128)S(1)} %get-tuple-element.25), channel_id=1, source_target_pairs={{0,1},{1,0},{2,3},{3,2},{4,5},{5,4},{6,7},{7,6},{8,9},{9,8},{10,11... | collective-permute-start | bytes 968 | tf_op jit(solution)/shard_map/ppermute | solution.py:30
  81.0 12.5 %collective-permute-start.1 = (s32[4,1,20]{2,1,0:T(1,128)S(1)}, s32[4,1,20]{2,1,0:T(1,128)S(1)}, u32[]{:S(2)}, u32[]{:S(2)}) collective-permute-start(s32[4,1,20]{2,1,0:T(1,128)S(1)} %get-tuple-element.24), channel_id=1, source_target_pairs={{0,2},{1,3},{2,0},{3,1},{4,6},{5,7},{6,4},{7,5},{8,10},{9,11},{10,... | collective-permute-start | bytes 968 | tf_op jit(solution)/shard_map/ppermute | solution.py:30
  114.6 5.9 %collective-permute-start.3 = (f32[4,1,128]{2,1,0:T(1,128)S(1)}, f32[4,1,128]{2,1,0:T(1,128)S(1)}, u32[]{:S(2)}, u32[]{:S(2)}) collective-permute-start(f32[4,1,128]{2,1,0:T(1,128)S(1)} %get-tuple-element.21), channel_id=1, source_target_pairs={{4,0},{8,4},{12,8},{5,1},{9,5},{13,9},{6,2},{10,6},{14,10},{7,3},{... | collective-permute-start | bytes 6152 | tf_op jit(solution)/shard_map/ppermute | solution.py:45
  115.9 5.8 %collective-permute-start.4 = (f32[4,1,128]{2,1,0:T(1,128)S(1)}, f32[4,1,128]{2,1,0:T(1,128)S(1)}, u32[]{:S(2)}, u32[]{:S(2)}) collective-permute-start(f32[4,1,128]{2,1,0:T(1,128)S(1)} %get-tuple-element.20), channel_id=1, source_target_pairs={{0,4},{4,8},{8,12},{1,5},{5,9},{9,13},{2,6},{6,10},{10,14},{3,7},{... | collective-permute-start | bytes 6152 | tf_op jit(solution)/shard_map/ppermute | solution.py:43
  121.9 6.0 %collective-permute-start.5 = (f32[4,18,1]{2,1,0:T(8,128)S(1)}, f32[4,18,1]{2,1,0:T(8,128)S(1)}, u32[]{:S(2)}, u32[]{:S(2)}) collective-permute-start(f32[4,18,1]{2,1,0:T(8,128)S(1)} %get-tuple-element.12), channel_id=1, source_target_pairs={{1,0},{2,1},{3,2},{5,4},{6,5},{7,6},{9,8},{10,9},{11,10},{13,12},{... | collective-permute-start | bytes 872 | tf_op jit(solution)/shard_map/ppermute | solution.py:45
  123.2 6.3 %collective-permute-start.6 = (f32[4,18,1]{2,1,0:T(8,128)S(1)}, f32[4,18,1]{2,1,0:T(8,128)S(1)}, u32[]{:S(2)}, u32[]{:S(2)}) collective-permute-start(f32[4,18,1]{2,1,0:T(8,128)S(1)} %get-tuple-element.13), channel_id=1, source_target_pairs={{0,1},{1,2},{2,3},{4,5},{5,6},{6,7},{8,9},{9,10},{10,11},{12,13},{... | collective-permute-start | bytes 872 | tf_op jit(solution)/shard_map/ppermute | solution.py:43
  129.6 50.7 %copy-start.1 = (f32[4,16,128]{2,1,0:T(8,128)S(1)}, f32[4,16,128]{2,1,0:T(8,128)}, u32[]{:S(2)}) copy-start(f32[4,16,128]{2,1,0:T(8,128)} %param.9) | copy-start | bytes 98308
  129.6 6.5 %collective-permute-start.7 = (f32[4,1,128]{2,1,0:T(1,128)S(1)}, f32[4,1,128]{2,1,0:T(1,128)S(1)}, u32[]{:S(2)}, u32[]{:S(2)}) collective-permute-start(f32[4,1,128]{2,1,0:T(1,128)S(1)} %get-tuple-element.19), channel_id=1, source_target_pairs={{4,0},{8,4},{12,8},{5,1},{9,5},{13,9},{6,2},{10,6},{14,10},{7,3},{... | collective-permute-start | bytes 6152 | tf_op jit(solution)/shard_map/ppermute | solution.py:45
  130.9 6.5 %collective-permute-start.8 = (f32[4,1,128]{2,1,0:T(1,128)S(1)}, f32[4,1,128]{2,1,0:T(1,128)S(1)}, u32[]{:S(2)}, u32[]{:S(2)}) collective-permute-start(f32[4,1,128]{2,1,0:T(1,128)S(1)} %get-tuple-element.18), channel_id=1, source_target_pairs={{0,4},{4,8},{8,12},{1,5},{5,9},{9,13},{2,6},{6,10},{10,14},{3,7},{... | collective-permute-start | bytes 6152 | tf_op jit(solution)/shard_map/ppermute | solution.py:43
  137.4 6.0 %collective-permute-start.10 = (f32[4,18,1]{2,1,0:T(8,128)S(1)}, f32[4,18,1]{2,1,0:T(8,128)S(1)}, u32[]{:S(2)}, u32[]{:S(2)}) collective-permute-start(f32[4,18,1]{2,1,0:T(8,128)S(1)} %get-tuple-element.11), channel_id=1, source_target_pairs={{0,1},{1,2},{2,3},{4,5},{5,6},{6,7},{8,9},{9,10},{10,11},{12,13},{... | collective-permute-start | bytes 872 | tf_op jit(solution)/shard_map/ppermute | solution.py:43
  141.7 6.0 %collective-permute-start.9 = (f32[4,18,1]{2,1,0:T(8,128)S(1)}, f32[4,18,1]{2,1,0:T(8,128)S(1)}, u32[]{:S(2)}, u32[]{:S(2)}) collective-permute-start(f32[4,18,1]{2,1,0:T(8,128)S(1)} %get-tuple-element.10), channel_id=1, source_target_pairs={{1,0},{2,1},{3,2},{5,4},{6,5},{7,6},{9,8},{10,9},{11,10},{13,12},{... | collective-permute-start | bytes 872 | tf_op jit(solution)/shard_map/ppermute | solution.py:45
  147.8 7.0 %collective-permute-start.11 = (f32[4,1,128]{2,1,0:T(1,128)S(1)}, f32[4,1,128]{2,1,0:T(1,128)S(1)}, u32[]{:S(2)}, u32[]{:S(2)}) collective-permute-start(f32[4,1,128]{2,1,0:T(1,128)S(1)} %get-tuple-element.17), channel_id=1, source_target_pairs={{4,0},{8,4},{12,8},{5,1},{9,5},{13,9},{6,2},{10,6},{14,10},{7,3},{... | collective-permute-start | bytes 6152 | tf_op jit(solution)/shard_map/ppermute | solution.py:45
  149.1 7.0 %collective-permute-start.12 = (f32[4,1,128]{2,1,0:T(1,128)S(1)}, f32[4,1,128]{2,1,0:T(1,128)S(1)}, u32[]{:S(2)}, u32[]{:S(2)}) collective-permute-start(f32[4,1,128]{2,1,0:T(1,128)S(1)} %get-tuple-element.16), channel_id=1, source_target_pairs={{0,4},{4,8},{8,12},{1,5},{5,9},{9,13},{2,6},{6,10},{10,14},{3,7},{... | collective-permute-start | bytes 6152 | tf_op jit(solution)/shard_map/ppermute | solution.py:43
  156.2 6.0 %collective-permute-start.13 = (f32[4,18,1]{2,1,0:T(8,128)S(1)}, f32[4,18,1]{2,1,0:T(8,128)S(1)}, u32[]{:S(2)}, u32[]{:S(2)}) collective-permute-start(f32[4,18,1]{2,1,0:T(8,128)S(1)} %get-tuple-element.8), channel_id=1, source_target_pairs={{1,0},{2,1},{3,2},{5,4},{6,5},{7,6},{9,8},{10,9},{11,10},{13,12},{... | collective-permute-start | bytes 872 | tf_op jit(solution)/shard_map/ppermute | solution.py:45
  157.5 6.3 %collective-permute-start.14 = (f32[4,18,1]{2,1,0:T(8,128)S(1)}, f32[4,18,1]{2,1,0:T(8,128)S(1)}, u32[]{:S(2)}, u32[]{:S(2)}) collective-permute-start(f32[4,18,1]{2,1,0:T(8,128)S(1)} %get-tuple-element.9), channel_id=1, source_target_pairs={{0,1},{1,2},{2,3},{4,5},{5,6},{6,7},{8,9},{9,10},{10,11},{12,13},{... | collective-permute-start | bytes 872 | tf_op jit(solution)/shard_map/ppermute | solution.py:43
  163.9 7.0 %collective-permute-start.15 = (f32[4,1,128]{2,1,0:T(1,128)S(1)}, f32[4,1,128]{2,1,0:T(1,128)S(1)}, u32[]{:S(2)}, u32[]{:S(2)}) collective-permute-start(f32[4,1,128]{2,1,0:T(1,128)S(1)} %get-tuple-element.15), channel_id=1, source_target_pairs={{4,0},{8,4},{12,8},{5,1},{9,5},{13,9},{6,2},{10,6},{14,10},{7,3},{... | collective-permute-start | bytes 6152 | tf_op jit(solution)/shard_map/ppermute | solution.py:45
  165.2 7.0 %collective-permute-start.16 = (f32[4,1,128]{2,1,0:T(1,128)S(1)}, f32[4,1,128]{2,1,0:T(1,128)S(1)}, u32[]{:S(2)}, u32[]{:S(2)}) collective-permute-start(f32[4,1,128]{2,1,0:T(1,128)S(1)} %get-tuple-element.14), channel_id=1, source_target_pairs={{0,4},{4,8},{8,12},{1,5},{5,9},{9,13},{2,6},{6,10},{10,14},{3,7},{... | collective-permute-start | bytes 6152 | tf_op jit(solution)/shard_map/ppermute | solution.py:43
  172.3 6.3 %collective-permute-start.17 = (f32[4,18,1]{2,1,0:T(8,128)S(1)}, f32[4,18,1]{2,1,0:T(8,128)S(1)}, u32[]{:S(2)}, u32[]{:S(2)}) collective-permute-start(f32[4,18,1]{2,1,0:T(8,128)S(1)} %get-tuple-element.6), channel_id=1, source_target_pairs={{1,0},{2,1},{3,2},{5,4},{6,5},{7,6},{9,8},{10,9},{11,10},{13,12},{... | collective-permute-start | bytes 872 | tf_op jit(solution)/shard_map/ppermute | solution.py:45
  173.6 6.6 %collective-permute-start.18 = (f32[4,18,1]{2,1,0:T(8,128)S(1)}, f32[4,18,1]{2,1,0:T(8,128)S(1)}, u32[]{:S(2)}, u32[]{:S(2)}) collective-permute-start(f32[4,18,1]{2,1,0:T(8,128)S(1)} %get-tuple-element.7), channel_id=1, source_target_pairs={{0,1},{1,2},{2,3},{4,5},{5,6},{6,7},{8,9},{9,10},{10,11},{12,13},{... | collective-permute-start | bytes 872 | tf_op jit(solution)/shard_map/ppermute | solution.py:43
  197.5 6.1 %copy-start.2 = (s32[1,1,1,256]{3,2,1,0:T(1,128)S(1)}, s32[1,1,1,256]{3,2,1,0:T(1,128)}, u32[]{:S(2)}) copy-start(s32[1,1,1,256]{3,2,1,0:T(1,128)} %param.7) | copy-start | bytes 3076
  197.5 17.8 %all-to-all-start.6 = ((bf16[4,4,20,4,2,128]{5,4,3,2,0,1:T(2,128)(2,1)}), bf16[4,4,20,4,2,128]{5,4,3,2,0,1:T(2,128)(2,1)S(1)}, u32[]{:S(2)}, u32[]{:S(2)}) async-start(bf16[4,4,20,4,2,128]{5,4,3,2,0,1:T(2,128)(2,1)} %copy.64), calls=%async_computation.6 | async-start | bytes 1310720 | tf_op jit(solution)/shard_map/all_to_all | solution.py:87
Sparse Core Ops, SparseCore 0:
  98.8 14.9 all-reduce.6
